TPU v7x, 32 devices: a whole 2x2x4 slice. The times are simulated.
32 devices in a mesh: leaf: 8 (over z, y), panel: 4 (over x, core).
Axes of the slice: x: 2, y: 2, z: 4, core: 2. Of those that a mesh axis runs over, the one named last changes fastest.
Arguments:
- interface_block: float32 [8, 2048, 2048], P('leaf', 'panel'), may hold values from -0.125 to 0.125
- coupling: bfloat16 [8, 2048, 128], P('leaf', 'panel'), may hold values from -0.375 to 0.375
- eigenvalues: float32 [8, 128], P('leaf'), may hold values from 0.5 to 8
- mode_counts: int32 [8], P('leaf'), may hold values from 64 to 128, as said below
- interface_coords: bfloat16 [8, 2048, 1024], P('leaf', 'panel'), may hold values from -6 to 6
- modal_coords: bfloat16 [8, 128, 4096], P('leaf'), may hold values from -6 to 6
Outputs:
- mode_shapes: float32 [8, 2048, 1024], P('leaf', 'panel')
Inputs may be any that keep to these rules, and one draw needn't show every extreme that they name: `mode_counts`: modes kept by each substructure; some substructure keeps all 128.
All inputs are finite; a program needn't handle non-finite values.
Results may differ from a plain program's by a relative error of at most 0.0023.
Values may be sent and summed in bfloat16 or wider, within the bound.
No kernel may reach another device: no remote copies, remote signals or barrier semaphores. Data moves between devices by JAX's collectives and lax.ppermute only.
A program may use at most 128 MiB of HBM per device.

v0:
```python
import jax
import jax.numpy as jnp
from jax import lax
from jax.sharding import Mesh, PartitionSpec as P


def on_device(interface_block, coupling, eigenvalues, mode_counts, interface_coords, modal_coords):
    block = interface_block[0]
    coup = coupling[0]
    coords = interface_coords[0]
    modal = modal_coords[0]
    width = coup.shape[1]
    group = lax.axis_size("leafin")
    index = jnp.arange(width, dtype=jnp.int32)
    mask = (index < mode_counts[0]).astype(jnp.float32)
    scaled = (coup.astype(jnp.float32) * (mask / eigenvalues[0])[None, :]).astype(jnp.bfloat16)
    dense = lax.psum(block, "leafin")
    scaled_all = lax.all_gather(scaled, "leafin", axis=1, tiled=True)
    coup_rows = lax.all_gather(coup, "panel", axis=0, tiled=True)
    coup_all = lax.all_gather(coup_rows, "leafin", axis=1, tiled=True)
    low = lax.dot_general(
        scaled_all, coup_all, (((1,), (1,)), ((), ())), preferred_element_type=jnp.float32
    )
    merged = dense - low
    rl = modal.shape[1] // group
    parts = jnp.transpose(modal.reshape(modal.shape[0], group, rl), (1, 0, 2))
    recv = lax.all_to_all(parts, "leafin", 0, 0, tiled=True)
    modal_term = jnp.dot(
        scaled_all, recv.reshape(group * modal.shape[0], rl), preferred_element_type=jnp.float32
    )
    coords_all = lax.all_gather(coords, "panel", axis=0, tiled=True)
    shapes = modal_term + jnp.dot(
        merged, coords_all.astype(jnp.float32), precision=lax.Precision.HIGHEST
    )
    return shapes[None]


def solution(mesh):

    def run(*args):
        group = args[5].shape[2] // args[4].shape[2]
        leaves, panels = (mesh.shape["leaf"], mesh.shape["panel"])
        grid = mesh.devices.reshape(leaves // group, group, panels)
        sub = Mesh(grid, ("grp", "leafin", "panel"))
        leaf = ("grp", "leafin")
        placed = (
            P(leaf, "panel", None),
            P(leaf, "panel", None),
            P(leaf, None),
            P(leaf),
            P(leaf, "panel", None),
            P(leaf, None, None),
        )
        body = jax.shard_map(
            on_device, mesh=sub, in_specs=placed, out_specs=P(leaf, "panel", None), check_vma=False
        )
        return body(*args)

    return run
```

profile of v0, /device:TPU:0, one launch (start us, length us, event | category | flops | bytes accessed | tf_op | source)
XLA Modules:
  0.0 295.3 jit_solution(14571388144809049129)
XLA Ops:
  6.5 0.0 copy-start
  6.5 0.0 all-gather.6.cloned.1.call-start
  6.5 10.3 %all-gather = bf16[1,2048,128]{2,1,0:T(8,128)(2,1)} all-gather(bf16[1,512,128]{2,1,0:T(8,128)(2,1)} %param.7), channel_id=2, replica_groups=mesh['grp'=2,'leafin'=4,'panel'=4] {'panel'}, dimensions={1}, use_global_device_ids=true | all-gather | bytes 655360 | tf_op jit(solution)/shard_map/all_gather | solution.py:19
  16.9 0.0 all-gather.6.cloned.1.call-update
  16.9 0.0 all-reduce.2.cloned.1.call-start
  16.9 0.0 copy-start.2
  16.9 0.0 copy-start.1
  17.0 0.7 all-reduce.2.cloned.1.call-update
  17.6 0.0 all-gather.8.cloned.1.call-start
  17.7 0.7 all-gather.8.cloned.1.call-update
  18.4 0.0 copy-done
  18.4 1.3 copy.7
  19.7 3.8 %all-to-all-start = ((bf16[4,128,1024]{1,2,0:T(8,128)(2,1)}), bf16[4,128,1024]{1,2,0:T(8,128)(2,1)S(1)}, u32[]{:S(2)}, u32[]{:S(2)}) async-start(bf16[4,128,1024]{1,2,0:T(8,128)(2,1)} %bitcast.4), calls=%async_computation | async-start | bytes 2097152 | tf_op jit(solution)/shard_map/all_to_all | solution.py:27
  24.1 0.0 copy-done.2
  24.2 0.0 copy-done.1
  24.2 57.9 %all_gather.12 = bf16[512,512]{1,0:T(8,128)(2,1)S(1)} all-gather(bf16[512,128]{1,0:T(8,128)(2,1)S(1)} %fusion.5), channel_id=1, replica_groups=mesh['grp'=2,'leafin'=4,'panel'=4] {'leafin'}, dimensions={1}, use_global_device_ids=true | all-gather | bytes 655360 | tf_op jit(solution)/shard_map/all_gather | solution.py:18
  82.1 0.0 all-to-all-done
  82.1 0.5 copy.8
  82.6 0.0 all-gather.6.cloned.1.call-done
  82.7 4.8 %fusion.3 = f32[512,2048]{1,0:T(8,128)} fusion(bf16[512,512]{1,0:T(8,128)(2,1)S(1)} %all_gather.12, bf16[1,2048,512]{2,1,0:T(8,128)(2,1)} %all-gather.6.cloned.1.call-done), kind=kOutput, calls=%fused_computation.3 | convolution fusion | flops 1073741824 | bytes 6815744 | tf_op jit(solution)/shard_map/dot_general | solution.py:21
  87.5 152.8 %all-reduce.2.cloned.1.call-done = f32[512,2048]{1,0:T(8,128)} async-done(((f32[512,2048]{1,0:T(8,128)}), f32[512,2048]{1,0:T(8,128)}) %all-reduce.2.cloned.1.call-update) | async-done | bytes 4194320 | tf_op jit(solution)/shard_map/psum | solution.py:17
  240.3 35.9 %all-gather.8.cloned.1.call-done = bf16[1,2048,1024]{2,1,0:T(8,128)(2,1)} async-done(((bf16[1,512,1024]{2,1,0:T(8,128)(2,1)}), bf16[1,2048,1024]{2,1,0:T(8,128)(2,1)}) %all-gather.8.cloned.1.call-update) | async-done | bytes 4194320 | tf_op jit(solution)/shard_map/all_gather | solution.py:31
  276.3 10.5 %fusion = f32[512,1024]{1,0:T(8,128)S(1)} fusion(bf16[1,2048,1024]{2,1,0:T(8,128)(2,1)} %all-gather.8.cloned.1.call-done, f32[512,2048]{1,0:T(8,128)} %all-reduce.2.cloned.1.call-done, f32[512,2048]{1,0:T(8,128)} %fusion.3), kind=kOutput, calls=%fused_computation | convolution fusion | flops 12885950464 | bytes 14680064 | tf_op jit(solution)/shard_map/dot_general | solution.py:32
  286.7 2.0 add_bitcast_fusion
  (2 shorter events, 0.0 us)
Async XLA Ops:
  6.5 11.8 %copy-start = (bf16[1,128,4096]{2,1,0:T(8,128)(2,1)S(1)}, bf16[1,128,4096]{2,1,0:T(8,128)(2,1)}, u32[]{:S(2)}) copy-start(bf16[1,128,4096]{2,1,0:T(8,128)(2,1)} %param.11) | copy-start | bytes 3145732
  6.5 76.1 %all-gather.6.cloned.1.call-start = ((), (), s32[]{:S(2)}) async-start(), calls=%async_computation.2 | async-start | bytes 2621440 | tf_op jit(solution)/shard_map/all_gather | solution.py:20
  16.9 223.5 %all-reduce.2.cloned.1.call-start = ((), (), s32[]{:S(2)}) async-start(), calls=%async_computation.1 | async-start | bytes 8388608 | tf_op jit(solution)/shard_map/psum | solution.py:17
  16.9 7.2 %copy-start.2 = (f32[1,128]{1,0:T(1,128)S(1)}, f32[1,128]{1,0:T(1,128)}, u32[]{:S(2)}) copy-start(f32[1,128]{1,0:T(1,128)} %param.8) | copy-start | bytes 1540
  16.9 7.2 %copy-start.1 = (bf16[1,512,128]{2,1,0:T(8,128)(2,1)S(1)}, bf16[1,512,128]{2,1,0:T(8,128)(2,1)}, u32[]{:S(2)}) copy-start(bf16[1,512,128]{2,1,0:T(8,128)(2,1)} %param.7) | copy-start | bytes 393220
  17.6 258.6 %all-gather.8.cloned.1.call-start = ((), (), s32[]{:S(2)}) async-start(), calls=%async_computation.3 | async-start | bytes 5242880 | tf_op jit(solution)/shard_map/all_gather | solution.py:31
  19.7 62.4 %all-to-all-start = ((bf16[4,128,1024]{1,2,0:T(8,128)(2,1)}), bf16[4,128,1024]{1,2,0:T(8,128)(2,1)S(1)}, u32[]{:S(2)}, u32[]{:S(2)}) async-start(bf16[4,128,1024]{1,2,0:T(8,128)(2,1)} %bitcast.4), calls=%async_computation | async-start | bytes 2097152 | tf_op jit(solution)/shard_map/all_to_all | solution.py:27
Sparse Core Ops, SparseCore 0:
  17.0 65.2 all-gather.5
  84.7 155.6 all-reduce.1
  241.9 34.2 all-gather.7
where the time goes:
time: 296 us; the launch traced here: 295 us
  waiting for transfers between devices  190 us (64%)
  blocking collectives  68.2 us (23%)
  matrix products  17.3 us (6%)
  between operations  13.8 us (5%)
  starting transfers between devices  3.88 us (1%)
    psum x1, waiting for transfers between devices, on_device(): dense = lax.psum(block, 'leafin')  153 us
    all_gather x1, blocking collectives, on_device(): scaled_all = lax.all_gather(scaled, 'leafin', axis=1, tiled=True)  57.9 us
    all_gather x1, waiting for transfers between devices, on_device(): coords_all = lax.all_gather(coords, 'panel', axis=0, tiled=True)  35.9 us
    dot_general x1, matrix products, on_device(): jnp.dot(merged, coords_all.astype(jnp.float32), precision=lax.Precision.H...  10.5 us
    all_gather x1, blocking collectives, on_device(): coup_rows = lax.all_gather(coup, 'panel', axis=0, tiled=True)  10.3 us
  transfers between devices with their start and end apart: 4, of which 2 were waited for; matrix products, arithmetic and copies ran while one was open for 2% of the time, Pallas kernels for 0%

commit v1 on v0

--- a/solution.py
+++ b/solution.py
@@ -2,6 +2,7 @@
 import jax.numpy as jnp
 from jax import lax
 from jax.sharding import Mesh, PartitionSpec as P
+from jax.lax import all_gather
 
 
 def on_device(interface_block, coupling, eigenvalues, mode_counts, interface_coords, modal_coords):
@@ -14,7 +15,7 @@
     index = jnp.arange(width, dtype=jnp.int32)
     mask = (index < mode_counts[0]).astype(jnp.float32)
     scaled = (coup.astype(jnp.float32) * (mask / eigenvalues[0])[None, :]).astype(jnp.bfloat16)
-    dense = lax.psum(block, "leafin")
+    dense = jnp.sum(all_gather(block, "leafin"), 0)
     scaled_all = lax.all_gather(scaled, "leafin", axis=1, tiled=True)
     coup_rows = lax.all_gather(coup, "panel", axis=0, tiled=True)
     coup_all = lax.all_gather(coup_rows, "leafin", axis=1, tiled=True)

time: 296 us -> 425 us (1.44)
  waiting for transfers between devices: 190 us -> 309 us
  other arithmetic: 0.04 us -> 10.4 us
    all_gather x0 -> x1, waiting for transfers between devices: none -> 283 us  [on_device(): dense = jnp.sum(all_gather(block, 'leafin'), 0)]
    psum x1 -> x0, waiting for transfers between devices: 153 us -> none  [on_device(): dense = lax.psum(block, 'leafin')]
    all_gather x1, waiting for transfers between devices: 35.9 us -> 24.8 us  [on_device(): coords_all = lax.all_gather(coords, 'panel', axis=0, tiled=True)]
    reduce_sum x0 -> x1, other arithmetic: none -> 10.3 us  [on_device(): dense = jnp.sum(all_gather(block, 'leafin'), 0)]
  transfers between devices with their start and end apart: 4 -> 4, of which waited for: 2 -> 2; matrix products, arithmetic and copies ran while one was open for 2% -> 4% of each run, Pallas kernels for 0% -> 0%
where the time goes in v1:
time: 425 us
  waiting for transfers between devices  309 us (73%)
  blocking collectives  68.2 us (16%)
  matrix products  17.3 us (4%)
  between operations  13.8 us (3%)
  other arithmetic  10.4 us (2%)
    all_gather x1, waiting for transfers between devices, on_device(): dense = jnp.sum(all_gather(block, 'leafin'), 0)  283 us
    all_gather x1, blocking collectives, on_device(): scaled_all = lax.all_gather(scaled, 'leafin', axis=1, tiled=True)  57.9 us
    all_gather x1, waiting for transfers between devices, on_device(): coords_all = lax.all_gather(coords, 'panel', axis=0, tiled=True)  24.8 us
    dot_general x1, matrix products, on_device(): jnp.dot(merged, coords_all.astype(jnp.float32), precision=lax.Precision.H...  10.5 us
    reduce_sum x1, other arithmetic, on_device(): dense = jnp.sum(all_gather(block, 'leafin'), 0)  10.3 us
    all_gather x1, blocking collectives, on_device(): coup_rows = lax.all_gather(coup, 'panel', axis=0, tiled=True)  10.3 us
  transfers between devices with their start and end apart: 4, of which 2 were waited for; matrix products, arithmetic and copies ran while one was open for 4% of the time, Pallas kernels for 0%

profile of v1, /device:TPU:0, one launch (start us, length us, event | category | flops | bytes accessed | tf_op | source)
XLA Modules:
  0.0 424.8 jit_solution(6572633663323587576)
XLA Ops:
  6.5 0.0 copy-start
  6.5 0.0 all-gather.9.cloned.1.call-start
  6.5 10.3 %all-gather = bf16[1,2048,128]{2,1,0:T(8,128)(2,1)} all-gather(bf16[1,512,128]{2,1,0:T(8,128)(2,1)} %param.7), channel_id=2, replica_groups=mesh['grp'=2,'leafin'=4,'panel'=4] {'panel'}, dimensions={1}, use_global_device_ids=true | all-gather | bytes 655360 | tf_op jit(solution)/shard_map/all_gather | solution.py:20
  16.9 0.0 all-gather.9.cloned.1.call-update
  16.9 0.0 copy-start.2
  16.9 0.0 copy-start.1
  16.9 0.0 all-gather.7.cloned.1.call-start
  16.9 0.7 all-gather.7.cloned.1.call-update
  17.7 0.0 all-gather.11.cloned.1.call-start
  17.7 0.7 all-gather.11.cloned.1.call-update
  18.4 0.0 copy-done
  18.4 1.3 copy.9
  19.7 3.8 all-to-all-start
  24.2 0.0 copy-done.2
  24.2 0.0 copy-done.1
  24.2 57.9 %all_gather.15 = bf16[512,512]{1,0:T(8,128)(2,1)S(1)} all-gather(bf16[512,128]{1,0:T(8,128)(2,1)S(1)} %fusion.5), channel_id=1, replica_groups=mesh['grp'=2,'leafin'=4,'panel'=4] {'leafin'}, dimensions={1}, use_global_device_ids=true | all-gather | bytes 655360 | tf_op jit(solution)/shard_map/all_gather | solution.py:19
  82.1 0.0 all-to-all-done
  82.1 0.5 copy.10
  82.7 0.0 all-gather.9.cloned.1.call-done
  82.7 4.8 %fusion.3 = f32[512,2048]{1,0:T(8,128)} fusion(bf16[512,512]{1,0:T(8,128)(2,1)S(1)} %all_gather.15, bf16[1,2048,512]{2,1,0:T(8,128)(2,1)} %all-gather.9.cloned.1.call-done), kind=kOutput, calls=%fused_computation.3 | convolution fusion | flops 1073741824 | bytes 6815744 | tf_op jit(solution)/shard_map/dot_general | solution.py:22
  87.5 283.1 %all-gather.7.cloned.1.call-done = f32[4,512,2048]{2,1,0:T(8,128)} async-done(((f32[1,512,2048]{2,1,0:T(8,128)}), f32[4,512,2048]{2,1,0:T(8,128)}) %all-gather.7.cloned.1.call-update) | async-done | bytes 16777232 | tf_op jit(solution)/shard_map/all_gather | solution.py:18
  370.7 10.3 %reduce_sum.9 = f32[512,2048]{1,0:T(8,128)} reduce(f32[4,512,2048]{2,1,0:T(8,128)} %all-gather.7.cloned.1.call-done, f32[]{:T(128)} %constant.0.clone.1), dimensions={0}, to_apply=%region_0.0 | reduce | flops 3145728 | bytes 20971524 | tf_op jit(solution)/shard_map/reduce_sum | solution.py:18
  381.0 24.8 %all-gather.11.cloned.1.call-done = bf16[1,2048,1024]{2,1,0:T(8,128)(2,1)} async-done(((bf16[1,512,1024]{2,1,0:T(8,128)(2,1)}), bf16[1,2048,1024]{2,1,0:T(8,128)(2,1)}) %all-gather.11.cloned.1.call-update) | async-done | bytes 4194320 | tf_op jit(solution)/shard_map/all_gather | solution.py:32
  405.8 10.5 %fusion = f32[512,1024]{1,0:T(8,128)S(1)} fusion(bf16[1,2048,1024]{2,1,0:T(8,128)(2,1)} %all-gather.11.cloned.1.call-done, f32[512,2048]{1,0:T(8,128)} %reduce_sum.9, f32[512,2048]{1,0:T(8,128)} %fusion.3), kind=kOutput, calls=%fused_computation | convolution fusion | flops 12885950464 | bytes 14680064 | tf_op jit(solution)/shard_map/dot_general | solution.py:33
  416.3 2.0 add_bitcast_fusion
  (2 shorter events, 0.0 us)
Async XLA Ops:
  6.5 11.9 %copy-start = (bf16[1,128,4096]{2,1,0:T(8,128)(2,1)S(1)}, bf16[1,128,4096]{2,1,0:T(8,128)(2,1)}, u32[]{:S(2)}) copy-start(bf16[1,128,4096]{2,1,0:T(8,128)(2,1)} %param.11) | copy-start | bytes 3145732
  6.5 76.1 %all-gather.9.cloned.1.call-start = ((), (), s32[]{:S(2)}) async-start(), calls=%async_computation.2 | async-start | bytes 2621440 | tf_op jit(solution)/shard_map/all_gather | solution.py:21
  16.9 7.3 %copy-start.2 = (f32[1,128]{1,0:T(1,128)S(1)}, f32[1,128]{1,0:T(1,128)}, u32[]{:S(2)}) copy-start(f32[1,128]{1,0:T(1,128)} %param.8) | copy-start | bytes 1540
  16.9 7.3 %copy-start.1 = (bf16[1,512,128]{2,1,0:T(8,128)(2,1)S(1)}, bf16[1,512,128]{2,1,0:T(8,128)(2,1)}, u32[]{:S(2)}) copy-start(bf16[1,512,128]{2,1,0:T(8,128)(2,1)} %param.7) | copy-start | bytes 393220
  16.9 353.8 %all-gather.7.cloned.1.call-start = ((), (), s32[]{:S(2)}) async-start(), calls=%async_computation.1 | async-start | bytes 20971520 | tf_op jit(solution)/shard_map/all_gather | solution.py:18
  17.7 388.2 %all-gather.11.cloned.1.call-start = ((), (), s32[]{:S(2)}) async-start(), calls=%async_computation.3 | async-start | bytes 5242880 | tf_op jit(solution)/shard_map/all_gather | solution.py:32
  19.7 62.4 %all-to-all-start = ((bf16[4,128,1024]{1,2,0:T(8,128)(2,1)}), bf16[4,128,1024]{1,2,0:T(8,128)(2,1)S(1)}, u32[]{:S(2)}, u32[]{:S(2)}) async-start(bf16[4,128,1024]{1,2,0:T(8,128)(2,1)} %bitcast.4), calls=%async_computation | async-start | bytes 2097152 | tf_op jit(solution)/shard_map/all_to_all | solution.py:28
Sparse Core Ops, SparseCore 0:
  17.0 65.2 all-gather.8
  83.8 286.8 all-gather.6
  372.2 33.5 all-gather.10
